TPU v7x, 32 devices: a whole 2x2x4 slice. The times are simulated.
32 devices in a mesh: dp: 8 (over y, x, core), fsdp: 4 (over z).
Axes of the slice: x: 2, y: 2, z: 4, core: 2. Of those that a mesh axis runs over, the one named last changes fastest.
Arguments:
- tokens: bfloat16 [64, 256, 768], P(('dp', 'fsdp')), may hold values from -6 to 6
- band_waves: int32 [64, 13], P(('dp', 'fsdp')), may hold values from 0 to 128, as said below
- visible_slot: int32 [64, 256], P(('dp', 'fsdp')), may hold values from 0 to 1023, as said below
- wave_table: bfloat16 [128, 768], P(('dp', 'fsdp')), may hold values from -1.75 to 1.75
- norm1_gain: bfloat16 [768], P(('dp', 'fsdp')), may hold values from 0.5 to 1.5
- norm1_bias: bfloat16 [768], P(('dp', 'fsdp')), may hold values from -1.75 to 1.75
- qkv_weight: bfloat16 [768, 2304], P(('dp', 'fsdp')), may hold values from -0.3125 to 0.3125
- out_weight: bfloat16 [768, 768], P(('dp', 'fsdp')), may hold values from -0.875 to 0.875
- norm2_gain: bfloat16 [768], P(('dp', 'fsdp')), may hold values from 0.5 to 1.5
- norm2_bias: bfloat16 [768], P(('dp', 'fsdp')), may hold values from -1.75 to 1.75
- mlp_in: bfloat16 [768, 3072], P(('dp', 'fsdp')), may hold values from -0.21875 to 0.21875
- mlp_in_bias: bfloat16 [3072], P(('dp', 'fsdp')), may hold values from -3 to 3
- mlp_out: bfloat16 [3072, 768], P(('dp', 'fsdp')), may hold values from -0.15625 to 0.15625
- mlp_out_bias: bfloat16 [768], P(('dp', 'fsdp')), may hold values from -1.75 to 1.75
- dec_weight: bfloat16 [768, 512], P(('dp', 'fsdp')), may hold values from -0.21875 to 0.21875
- dec_bias: bfloat16 [512], P(('dp', 'fsdp')), may hold values from -1.75 to 1.75
- mask_token: bfloat16 [512], P(('dp', 'fsdp')), may hold values from -6 to 6
- cot_decoded: bfloat16 [64, 1024, 512], P(None, ('dp', 'fsdp')), may hold values from -6 to 6
Outputs:
- decoded: bfloat16 [64, 1024, 512], P(None, ('dp', 'fsdp'))
- grad_tokens: float32 [64, 256, 768], P(('dp', 'fsdp'))
- grad_wave_table: float32 [128, 768], P(('dp', 'fsdp'))
- grad_norm1_gain: float32 [768], P(('dp', 'fsdp'))
- grad_norm1_bias: float32 [768], P(('dp', 'fsdp'))
- grad_qkv_weight: float32 [768, 2304], P(('dp', 'fsdp'))
- grad_out_weight: float32 [768, 768], P(('dp', 'fsdp'))
- grad_norm2_gain: float32 [768], P(('dp', 'fsdp'))
- grad_norm2_bias: float32 [768], P(('dp', 'fsdp'))
- grad_mlp_in: float32 [768, 3072], P(('dp', 'fsdp'))
- grad_mlp_in_bias: float32 [3072], P(('dp', 'fsdp'))
- grad_mlp_out: float32 [3072, 768], P(('dp', 'fsdp'))
- grad_mlp_out_bias: float32 [768], P(('dp', 'fsdp'))
- grad_dec_weight: float32 [768, 512], P(('dp', 'fsdp'))
- grad_dec_bias: float32 [512], P(('dp', 'fsdp'))
- grad_mask_token: float32 [512], P(('dp', 'fsdp'))
Inputs may be any that keep to these rules, and one draw needn't show every extreme that they name: `band_waves`: the first 4 entries of a row are ids below 128; an entry equal to 128 marks an unused band slot, so a chip has 4 to 13 bands; ids may repeat. `visible_slot`: the 256 entries of a row are distinct; the other slots of that chip hold the mask token.
All inputs are finite; a program needn't handle non-finite values.
Results may differ from a plain program's by a relative error of at most 0.012.
The roundings to bfloat16 on the way count: a program that leaves them out, or rounds other values in their place, can miss the bound.
Values may be sent and summed in bfloat16 or wider, within the bound.
No kernel may reach another device: no remote copies, remote signals or barrier semaphores. Data moves between devices by JAX's collectives and lax.ppermute only.
A program may use at most 128 MiB of HBM per device.

v0:
```python
import jax
import jax.numpy as jnp
from jax import lax
from jax.sharding import PartitionSpec as P

D = 768
HD = 64
DEC = 512
WAVES = 128
L = 1024
NORM_EPSILON = 1e-05
ROOT_HALF = 0.7071067811865476
INVERSE_ROOT_TAU = 0.3989422804014327
HIGH_PRECISION = lax.Precision.HIGHEST


def product(left_op, right_op):
    return jnp.dot(left_op, right_op, preferred_element_type=jnp.float32)


def inner_rows(left_op, right_op):
    return lax.dot_general(
        left_op, right_op, (((0,), (0,)), ((), ())), preferred_element_type=jnp.float32
    )


def outer_cols(left_op, right_op):
    return lax.dot_general(
        left_op, right_op, (((1,), (1,)), ((), ())), preferred_element_type=jnp.float32
    )


def norm_forward(residual, gain, shift):
    mean_val = jnp.mean(residual, axis=-1, keepdims=True)
    centered = residual - mean_val
    variance = jnp.mean(centered * centered, axis=-1, keepdims=True)
    inverse = lax.rsqrt(variance + NORM_EPSILON)
    normed = centered * inverse
    return (normed * gain + shift, normed, inverse)


def norm_backward(incoming, normed, inverse, gain):
    scaled = incoming * gain
    first_mean = jnp.mean(scaled, axis=-1, keepdims=True)
    second_mean = jnp.mean(scaled * normed, axis=-1, keepdims=True)
    grad_input = inverse * (scaled - first_mean - normed * second_mean)
    return (grad_input, jnp.sum(incoming * normed, axis=0), jnp.sum(incoming, axis=0))


def gelu_value(hidden):
    return 0.5 * hidden * (1.0 + lax.erf(hidden * ROOT_HALF))


def gelu_slope(hidden):
    return (
        0.5 * (1.0 + lax.erf(hidden * ROOT_HALF))
        + hidden * jnp.exp(-0.5 * hidden * hidden) * INVERSE_ROOT_TAU
    )


def head_slice(source, pair_index):
    chip_count, vis_len, feature_width = source.shape
    piece = lax.dynamic_slice_in_dim(source, pair_index * 2 * HD, 2 * HD, axis=2)
    return piece.reshape(chip_count, vis_len, 2, HD)


def attend(queries, key_rows, value_rows):
    chip_count, vis_len, feature_width = queries.shape
    score_scale = HD ** (-0.5)

    def one_pair(pair_index):
        query_part = head_slice(queries, pair_index)
        key_part = head_slice(key_rows, pair_index)
        value_part = head_slice(value_rows, pair_index)
        scores = (
            jnp.einsum("cqhd,ckhd->chqk", query_part, key_part, preferred_element_type=jnp.float32)
            * score_scale
        )
        row_peak = jnp.max(scores, axis=-1, keepdims=True)
        exponents = jnp.exp(scores - row_peak)
        row_total = jnp.sum(exponents, axis=-1, keepdims=True)
        soft_weights = (exponents / row_total).astype(jnp.bfloat16)
        mixture = jnp.einsum(
            "chqk,ckhd->cqhd", soft_weights, value_part, preferred_element_type=jnp.float32
        )
        return (
            mixture.astype(jnp.bfloat16).reshape(chip_count, vis_len, 2 * HD),
            row_peak + jnp.log(row_total),
        )

    mixtures, log_totals = lax.map(one_pair, jnp.arange(feature_width // (2 * HD)))
    merged = mixtures.transpose(1, 2, 0, 3).reshape(chip_count * vis_len, feature_width)
    return (merged, log_totals)


def attend_back(queries, key_rows, value_rows, log_totals, grad_mixture):
    chip_count, vis_len, feature_width = queries.shape
    score_scale = HD ** (-0.5)
    part_shape = (chip_count, vis_len, 2 * HD)

    def one_pair(inputs):
        pair_index, log_total = inputs
        query_part = head_slice(queries, pair_index)
        key_part = head_slice(key_rows, pair_index)
        value_part = head_slice(value_rows, pair_index)
        grad_part = head_slice(grad_mixture, pair_index)
        scores = (
            jnp.einsum("cqhd,ckhd->chqk", query_part, key_part, preferred_element_type=jnp.float32)
            * score_scale
        )
        soft_full = jnp.exp(scores - log_total)
        soft_low = soft_full.astype(jnp.bfloat16)
        grad_values = jnp.einsum(
            "chqk,cqhd->ckhd", soft_low, grad_part, preferred_element_type=jnp.float32
        )
        grad_soft = jnp.einsum(
            "cqhd,ckhd->chqk", grad_part, value_part, preferred_element_type=jnp.float32
        )
        row_delta = jnp.sum(grad_soft * soft_full, axis=-1, keepdims=True)
        grad_scores = (soft_full * (grad_soft - row_delta)).astype(jnp.bfloat16)
        grad_queries = (
            jnp.einsum("chqk,ckhd->cqhd", grad_scores, key_part, preferred_element_type=jnp.float32)
            * score_scale
        )
        grad_keys = (
            jnp.einsum(
                "chqk,cqhd->ckhd", grad_scores, query_part, preferred_element_type=jnp.float32
            )
            * score_scale
        )
        return (
            grad_queries.reshape(part_shape),
            grad_keys.reshape(part_shape),
            grad_values.reshape(part_shape),
        )

    grad_q_all, grad_k_all, grad_v_all = lax.map(
        one_pair, (jnp.arange(feature_width // (2 * HD)), log_totals)
    )
    flat_rows = chip_count * vis_len
    return (
        grad_q_all.transpose(1, 2, 0, 3).reshape(flat_rows, feature_width),
        grad_k_all.transpose(1, 2, 0, 3).reshape(flat_rows, feature_width),
        grad_v_all.transpose(1, 2, 0, 3).reshape(flat_rows, feature_width),
    )


def local(
    tokens,
    band_waves,
    visible_slot,
    wave_table,
    norm1_gain,
    norm1_bias,
    qkv_weight,
    out_weight,
    norm2_gain,
    norm2_bias,
    mlp_in,
    mlp_in_bias,
    mlp_out,
    mlp_out_bias,
    dec_weight,
    dec_bias,
    mask_token,
    cot_decoded,
):
    shards = (
        wave_table,
        norm1_gain,
        norm1_bias,
        qkv_weight,
        out_weight,
        norm2_gain,
        norm2_bias,
        mlp_in,
        mlp_in_bias,
        mlp_out,
        mlp_out_bias,
        dec_weight,
        dec_bias,
        mask_token,
    )
    gathered = (
        lax.all_gather(shards[0], ("dp", "fsdp"), axis=0, tiled=True),
        lax.all_gather(shards[1], ("dp", "fsdp"), axis=0, tiled=True),
        lax.all_gather(shards[2], ("dp", "fsdp"), axis=0, tiled=True),
        lax.all_gather(shards[3], ("dp", "fsdp"), axis=0, tiled=True),
        lax.all_gather(shards[4], ("dp", "fsdp"), axis=0, tiled=True),
        lax.all_gather(shards[5], ("dp", "fsdp"), axis=0, tiled=True),
        lax.all_gather(shards[6], ("dp", "fsdp"), axis=0, tiled=True),
        lax.all_gather(shards[7], ("dp", "fsdp"), axis=0, tiled=True),
        lax.all_gather(shards[8], ("dp", "fsdp"), axis=0, tiled=True),
        lax.all_gather(shards[9], ("dp", "fsdp"), axis=0, tiled=True),
        lax.all_gather(shards[10], ("dp", "fsdp"), axis=0, tiled=True),
        lax.all_gather(shards[11], ("dp", "fsdp"), axis=0, tiled=True),
        lax.all_gather(shards[12], ("dp", "fsdp"), axis=0, tiled=True),
        lax.all_gather(shards[13], ("dp", "fsdp"), axis=0, tiled=True),
    )
    (
        wave_full,
        gain_one,
        shift_one,
        qkv_full,
        out_full,
        gain_two,
        shift_two,
        inner_full,
        inner_bias,
        outer_full,
        outer_bias,
        dec_full,
        dec_shift,
        mask_full,
    ) = gathered
    chip_count, vis_len, feature_width = tokens.shape
    row_count = chip_count * vis_len
    counts = jnp.sum(
        (band_waves[:, :, None] == jnp.arange(WAVES, dtype=jnp.int32)[None, None, :]).astype(
            jnp.float32
        ),
        axis=1,
    )
    spectral = jnp.dot(counts.astype(jnp.bfloat16), wave_full, preferred_element_type=jnp.float32)
    residual = (tokens.astype(jnp.float32) + spectral[:, None, :]).reshape(row_count, D)
    norm_out_one, normed_one, inverse_one = norm_forward(
        residual, gain_one.astype(jnp.float32), shift_one.astype(jnp.float32)
    )
    act_one = norm_out_one.astype(jnp.bfloat16)
    qkv_vals = product(act_one, qkv_full).astype(jnp.bfloat16)
    queries = qkv_vals[:, :D].reshape(chip_count, vis_len, D)
    key_rows = qkv_vals[:, D : 2 * D].reshape(chip_count, vis_len, D)
    value_rows = qkv_vals[:, 2 * D :].reshape(chip_count, vis_len, D)
    mixture, log_totals = attend(queries, key_rows, value_rows)
    res_one = residual + product(mixture, out_full)
    norm_out_two, normed_two, inverse_two = norm_forward(
        res_one, gain_two.astype(jnp.float32), shift_two.astype(jnp.float32)
    )
    act_two = norm_out_two.astype(jnp.bfloat16)
    hidden = product(act_two, inner_full) + inner_bias.astype(jnp.float32)
    active = gelu_value(hidden).astype(jnp.bfloat16)
    res_two = res_one + (product(active, outer_full) + outer_bias.astype(jnp.float32))
    enc_low = res_two.astype(jnp.bfloat16)
    projected = (product(enc_low, dec_full) + dec_shift.astype(jnp.float32)).astype(jnp.bfloat16)
    chip_index = jnp.arange(chip_count, dtype=jnp.int32)[:, None]
    filled = jnp.broadcast_to(mask_full, (chip_count, L, DEC))
    filled = filled.at[chip_index, visible_slot].set(projected.reshape(chip_count, vis_len, DEC))
    decoded = lax.all_to_all(filled, ("dp", "fsdp"), split_axis=1, concat_axis=0, tiled=True)
    grad_full = lax.all_to_all(cot_decoded, ("dp", "fsdp"), split_axis=0, concat_axis=1, tiled=True)
    back_weights = (
        lax.all_gather(shards[0], ("dp", "fsdp"), axis=0, tiled=True),
        lax.all_gather(shards[1], ("dp", "fsdp"), axis=0, tiled=True),
        lax.all_gather(shards[2], ("dp", "fsdp"), axis=0, tiled=True),
        lax.all_gather(shards[3], ("dp", "fsdp"), axis=0, tiled=True),
        lax.all_gather(shards[4], ("dp", "fsdp"), axis=0, tiled=True),
        lax.all_gather(shards[5], ("dp", "fsdp"), axis=0, tiled=True),
        lax.all_gather(shards[6], ("dp", "fsdp"), axis=0, tiled=True),
        lax.all_gather(shards[7], ("dp", "fsdp"), axis=0, tiled=True),
        lax.all_gather(shards[8], ("dp", "fsdp"), axis=0, tiled=True),
        lax.all_gather(shards[9], ("dp", "fsdp"), axis=0, tiled=True),
        lax.all_gather(shards[10], ("dp", "fsdp"), axis=0, tiled=True),
        lax.all_gather(shards[11], ("dp", "fsdp"), axis=0, tiled=True),
        lax.all_gather(shards[12], ("dp", "fsdp"), axis=0, tiled=True),
        lax.all_gather(shards[13], ("dp", "fsdp"), axis=0, tiled=True),
    )
    (
        unused_wave,
        back_gain_one,
        unused_shift_one,
        back_qkv,
        back_out,
        back_gain_two,
        unused_shift_two,
        back_inner,
        unused_inner_bias,
        back_outer,
        unused_outer_bias,
        back_dec,
        unused_dec_shift,
        unused_mask,
    ) = back_weights
    grad_vis_low = jnp.take_along_axis(grad_full, visible_slot[:, :, None], axis=1).reshape(
        row_count, DEC
    )
    grad_vis = grad_vis_low.astype(jnp.float32)
    grad_mask_token = jnp.sum(grad_full.astype(jnp.float32), axis=(0, 1)) - jnp.sum(
        grad_vis, axis=0
    )
    grad_dec_bias = jnp.sum(grad_vis, axis=0)
    grad_dec_weight = inner_rows(enc_low, grad_vis_low)
    grad_res_two = outer_cols(grad_vis_low, back_dec)
    grad_ffo = grad_res_two.astype(jnp.bfloat16)
    grad_mlp_out_bias = jnp.sum(grad_ffo.astype(jnp.float32), axis=0)
    grad_mlp_out = inner_rows(active, grad_ffo)
    grad_hidden = (outer_cols(grad_ffo, back_outer) * gelu_slope(hidden)).astype(jnp.bfloat16)
    grad_mlp_in_bias = jnp.sum(grad_hidden.astype(jnp.float32), axis=0)
    grad_mlp_in = inner_rows(act_two, grad_hidden)
    grad_act_two = outer_cols(grad_hidden, back_inner)
    grad_norm_two, grad_norm2_gain, grad_norm2_bias = norm_backward(
        grad_act_two, normed_two, inverse_two, back_gain_two.astype(jnp.float32)
    )
    grad_res_one = grad_res_two + grad_norm_two
    grad_att = grad_res_one.astype(jnp.bfloat16)
    grad_out_weight = inner_rows(mixture, grad_att)
    grad_mixed = outer_cols(grad_att, back_out).astype(jnp.bfloat16).reshape(chip_count, vis_len, D)
    grad_queries, grad_keys, grad_values = attend_back(
        queries, key_rows, value_rows, log_totals, grad_mixed
    )
    grad_qkv = jnp.concatenate([grad_queries, grad_keys, grad_values], axis=1).astype(jnp.bfloat16)
    grad_qkv_weight = inner_rows(act_one, grad_qkv)
    grad_act_one = outer_cols(grad_qkv, back_qkv)
    grad_norm_one, grad_norm1_gain, grad_norm1_bias = norm_backward(
        grad_act_one, normed_one, inverse_one, back_gain_one.astype(jnp.float32)
    )
    grad_tokens = (grad_res_one + grad_norm_one).reshape(chip_count, vis_len, D)
    chip_sums = jnp.sum(grad_tokens, axis=1)
    grad_wave_table = lax.dot_general(
        counts, chip_sums, (((0,), (0,)), ((), ())), precision=HIGH_PRECISION
    )
    local_grads = (
        grad_wave_table,
        grad_norm1_gain,
        grad_norm1_bias,
        grad_qkv_weight,
        grad_out_weight,
        grad_norm2_gain,
        grad_norm2_bias,
        grad_mlp_in,
        grad_mlp_in_bias,
        grad_mlp_out,
        grad_mlp_out_bias,
        grad_dec_weight,
        grad_dec_bias,
        grad_mask_token,
    )
    summed = (
        lax.psum_scatter(local_grads[0], ("dp", "fsdp"), scatter_dimension=0, tiled=True),
        lax.psum_scatter(local_grads[1], ("dp", "fsdp"), scatter_dimension=0, tiled=True),
        lax.psum_scatter(local_grads[2], ("dp", "fsdp"), scatter_dimension=0, tiled=True),
        lax.psum_scatter(local_grads[3], ("dp", "fsdp"), scatter_dimension=0, tiled=True),
        lax.psum_scatter(local_grads[4], ("dp", "fsdp"), scatter_dimension=0, tiled=True),
        lax.psum_scatter(local_grads[5], ("dp", "fsdp"), scatter_dimension=0, tiled=True),
        lax.psum_scatter(local_grads[6], ("dp", "fsdp"), scatter_dimension=0, tiled=True),
        lax.psum_scatter(local_grads[7], ("dp", "fsdp"), scatter_dimension=0, tiled=True),
        lax.psum_scatter(local_grads[8], ("dp", "fsdp"), scatter_dimension=0, tiled=True),
        lax.psum_scatter(local_grads[9], ("dp", "fsdp"), scatter_dimension=0, tiled=True),
        lax.psum_scatter(local_grads[10], ("dp", "fsdp"), scatter_dimension=0, tiled=True),
        lax.psum_scatter(local_grads[11], ("dp", "fsdp"), scatter_dimension=0, tiled=True),
        lax.psum_scatter(local_grads[12], ("dp", "fsdp"), scatter_dimension=0, tiled=True),
        lax.psum_scatter(local_grads[13], ("dp", "fsdp"), scatter_dimension=0, tiled=True),
    )
    return (
        decoded,
        grad_tokens,
        summed[0],
        summed[1],
        summed[2],
        summed[3],
        summed[4],
        summed[5],
        summed[6],
        summed[7],
        summed[8],
        summed[9],
        summed[10],
        summed[11],
        summed[12],
        summed[13],
    )


def solution(mesh):
    placed = (
        P(("dp", "fsdp"), None, None),
        P(("dp", "fsdp"), None),
        P(("dp", "fsdp"), None),
        P(("dp", "fsdp"), None),
        P(("dp", "fsdp")),
        P(("dp", "fsdp")),
        P(("dp", "fsdp"), None),
        P(("dp", "fsdp"), None),
        P(("dp", "fsdp")),
        P(("dp", "fsdp")),
        P(("dp", "fsdp"), None),
        P(("dp", "fsdp")),
        P(("dp", "fsdp"), None),
        P(("dp", "fsdp")),
        P(("dp", "fsdp"), None),
        P(("dp", "fsdp")),
        P(("dp", "fsdp")),
        P(None, ("dp", "fsdp"), None),
    )
    return jax.shard_map(
        local,
        mesh=mesh,
        in_specs=placed,
        out_specs=(
            P(None, ("dp", "fsdp"), None),
            P(("dp", "fsdp"), None, None),
            P(("dp", "fsdp"), None),
            P(("dp", "fsdp")),
            P(("dp", "fsdp")),
            P(("dp", "fsdp"), None),
            P(("dp", "fsdp"), None),
            P(("dp", "fsdp")),
            P(("dp", "fsdp")),
            P(("dp", "fsdp"), None),
            P(("dp", "fsdp")),
            P(("dp", "fsdp"), None),
            P(("dp", "fsdp")),
            P(("dp", "fsdp"), None),
            P(("dp", "fsdp")),
            P(("dp", "fsdp")),
        ),
        check_vma=False,
    )
```

profile of v0, /device:TPU:0, one launch (start us, length us, event | category | flops | bytes accessed | tf_op | source)
XLA Modules:
  0.0 1167.7 jit_solution(14192374103499020075)
XLA Ops:
  9.5 7.5 all-to-all-start.1
  17.7 123.0 %all-gather = bf16[32,4,768]{2,1,0:T(4,128)(2,1)S(1)} all-gather(bf16[1,4,768]{2,1,0:T(4,128)(2,1)S(1)} %bitcast.243), channel_id=1, replica_groups=mesh['dp'=8,'fsdp'=4] {'dp','fsdp'}, dimensions={0}, use_global_device_ids=true | all-gather | bytes 202752 | tf_op jit(solution)/shard_map/all_gather | solution.py:185
  142.8 37.7 %all-reduce.18 = (bf16[512]{0:T(512)(128)(2,1)S(1)}, bf16[768]{0:T(1024)(128)(2,1)S(1)}, bf16[768]{0:T(1024)(128)(2,1)S(1)}, bf16[768]{0:T(1024)(128)(2,1)S(1)},...) all-reduce(bf16[512]{0:T(512)(128)(2,1)S(1)} %dynamic-update-slice,, ...), channel_id=1, replica_groups=mesh['dp'=8,'fsdp'=4] {'dp','fsdp'}, use_global_device_ids=true, to_apply=%add | all-reduce | flops 7936 | bytes 31744
  182.8 83.6 %all_gather.61 = bf16[768,512]{1,0:T(8,128)(2,1)} all-gather(bf16[24,512]{1,0:T(8,128)(2,1)S(1)} %copy-done.19), channel_id=1, replica_groups=mesh['dp'=8,'fsdp'=4] {'dp','fsdp'}, dimensions={0}, use_global_device_ids=true | all-gather | bytes 811008 | tf_op jit(solution)/shard_map/all_gather | solution.py:196
  266.4 3.2 copy.128
  269.5 9.9 gather_fusion
  281.4 4.8 convolution_convert_fusion.1
  287.7 2.3 copy.121
  290.0 2.3 copy.122
  292.3 2.3 copy.123
  294.6 28.2 %while.30 = (s32[]{:T(128)}, bf16[6,2,256,128]{2,3,1,0:T(8,128)(2,1)}, f32[6,2,2,256,1]{3,2,1,4,0:T(2,128)S(1)}, s32[6]{0:T(128)S(1)}, bf16[2,256,768]{1,2,0:T(8...) while((s32[]{:T(128)}, ...), condition=%wide.region_6.7_spmd, body=%wide.region_3.6_spmd.sunk | while | flops 69008384 | bytes 4751551 | solution.py:91
  322.9 1.9 copy.124
  325.9 2.4 fusion.36
  329.8 8.4 multiply_convert_fusion.1
  338.1 7.5 convert_reduce_fusion
  345.6 3.1 multiply_reduce_fusion.1
  351.7 49.0 %while.31 = (s32[]{:T(128)}, bf16[6,2,256,128]{2,3,1,0:T(8,128)(2,1)}, bf16[6,2,256,128]{2,3,1,0:T(8,128)(2,1)}, bf16[6,2,256,128]{2,3,1,0:T(8,128)(2,1)}, s32[6...) while((s32[]{:T(128)}, ...), condition=%wide.region_14.15_spmd, body=%wide.region_12.14_spmd.sunk | while | flops 170130432 | bytes 11292899 | solution.py:137
  407.7 2.5 multiply_reduce_fusion.2
  413.6 6.0 add_convert_fusion
  422.3 3.3 fusion.14
  426.8 6.6 fusion.38
  433.5 7.2 fusion.32
  442.1 8.2 fusion.26
  452.4 26.7 %scatter_fusion = bf16[2,1024,512]{2,1,0:T(8,128)(2,1)S(1)} fusion(bf16[2,1024,512]{2,1,0:T(8,128)(2,1)S(1)} %broadcast_in_dim.84, s32[512]{0:T(512)S(1)} %bitcast.201, bf16[512,512]{1,0:T(8,128)(2,1)S(1)} %fusion.12), kind=kCustom, calls=%fused_computation.1 | custom fusion | bytes 1576960 | tf_op jit(solution)/shard_map/scatter | solution.py:247
  479.1 3.5 copy.125
  482.6 2.9 all-to-all-start
  487.6 68.5 %all-reduce.17 = (f32[768]{0:T(1024)S(1)}, f32[768]{0:T(1024)S(1)}, f32[768]{0:T(1024)S(1)}, f32[768]{0:T(1024)S(1)}, f32[3072]{0:T(1024)S(1)}, /*index=5*/f32[768]{0:T(1024)S(1)}, f32[512]{0:T(512)S(1)}, f32[512]{0:T(512)S(1)}) all-reduce(f32[768]{0:T(1024)S(1)} %get-tuple-element.342, ...), channel_id=3, replica_groups=mesh['dp'=8,'fsdp'=4] {'dp','fsdp'}, use_global_device_ids=true, to_apply=%region_20.21.clone | all-reduce | flops 7936 | bytes 63488
  564.1 84.0 %reduce-scatter.14.cloned.1.call-done = f32[24,512]{1,0:T(8,128)} async-done(((f32[768,512]{1,0:T(8,128)}), f32[24,512]{1,0:T(8,128)}) %reduce-scatter.14.cloned.1.call-update) | async-done | bytes 49168 | tf_op jit(solution)/shard_map/reduce_scatter | solution.py:348
  648.1 104.6 %reduce-scatter.8.cloned.1.call-done = f32[24,768]{1,0:T(8,128)} async-done(((f32[768,768]{1,0:T(8,128)}), f32[24,768]{1,0:T(8,128)}) %reduce-scatter.8.cloned.1.call-update) | async-done | bytes 73744 | tf_op jit(solution)/shard_map/reduce_scatter | solution.py:341
  752.6 124.8 %reduce-scatter.6.cloned.1.call-done = f32[24,2304]{1,0:T(8,128)} async-done(((f32[768,2304]{1,0:T(8,128)}), f32[24,2304]{1,0:T(8,128)}) %reduce-scatter.6.cloned.1.call-update) | async-done | bytes 221200 | tf_op jit(solution)/shard_map/reduce_scatter | solution.py:340
  877.5 141.6 %reduce-scatter.10.cloned.1.call-done = f32[24,3072]{1,0:T(8,128)} async-done(((f32[768,3072]{1,0:T(8,128)}), f32[24,3072]{1,0:T(8,128)}) %reduce-scatter.10.cloned.1.call-update) | async-done | bytes 294928 | tf_op jit(solution)/shard_map/reduce_scatter | solution.py:344
  1019.1 141.5 %reduce-scatter.12.cloned.1.call-done = f32[96,768]{1,0:T(8,128)} async-done(((f32[3072,768]{1,0:T(8,128)}), f32[96,768]{1,0:T(8,128)}) %reduce-scatter.12.cloned.1.call-update) | async-done | bytes 294928 | tf_op jit(solution)/shard_map/reduce_scatter | solution.py:346
  (319 shorter events, 112.4 us)
Async XLA Ops:
  7.2 274.2 %all-gather.6.cloned.1.call-start = ((), (), s32[]{:S(2)}) async-start(), calls=%async_computation.7 | async-start | bytes 3649536 | tf_op jit(solution)/shard_map/all_gather | solution.py:188
  7.9 317.9 %all-gather.8.cloned.1.call-start = ((), (), s32[]{:S(2)}) async-start(), calls=%async_computation.8 | async-start | bytes 1216512 | tf_op jit(solution)/shard_map/all_gather | solution.py:189
  8.7 321.1 %all-gather.10.cloned.1.call-start = ((), (), s32[]{:S(2)}) async-start(), calls=%async_computation.9 | async-start | bytes 4866048 | tf_op jit(solution)/shard_map/all_gather | solution.py:192
  9.4 8.3 copy-start.21
  9.4 131.4 %copy-start.22 = (s32[2,13]{1,0:T(2,128)S(1)}, s32[2,13]{1,0:T(2,128)}, u32[]{:S(2)}) copy-start(s32[2,13]{1,0:T(2,128)} %param.23) | copy-start | bytes 316
  9.4 131.5 %copy-start.25 = (bf16[24]{0:T(256)(128)(2,1)S(1)}, bf16[24]{0:T(256)(128)(2,1)}, u32[]{:S(2)}) copy-start(bf16[24]{0:T(256)(128)(2,1)} %param.27) | copy-start | bytes 148
  9.4 131.7 %copy-start.26 = (bf16[24]{0:T(256)(128)(2,1)S(1)}, bf16[24]{0:T(256)(128)(2,1)}, u32[]{:S(2)}) copy-start(bf16[24]{0:T(256)(128)(2,1)} %param.26) | copy-start | bytes 148
  9.4 131.9 %copy-start.27 = (bf16[24]{0:T(256)(128)(2,1)S(1)}, bf16[24]{0:T(256)(128)(2,1)}, u32[]{:S(2)}) copy-start(bf16[24]{0:T(256)(128)(2,1)} %param.31) | copy-start | bytes 148
  9.4 132.1 %copy-start.28 = (bf16[24]{0:T(256)(128)(2,1)S(1)}, bf16[24]{0:T(256)(128)(2,1)}, u32[]{:S(2)}) copy-start(bf16[24]{0:T(256)(128)(2,1)} %param.30) | copy-start | bytes 148
  9.5 132.4 %copy-start.29 = (bf16[24]{0:T(256)(128)(2,1)S(1)}, bf16[24]{0:T(256)(128)(2,1)}, u32[]{:S(2)}) copy-start(bf16[24]{0:T(256)(128)(2,1)} %param.35) | copy-start | bytes 148
  9.5 132.6 %copy-start.30 = (bf16[16]{0:T(256)(128)(2,1)S(1)}, bf16[16]{0:T(256)(128)(2,1)}, u32[]{:S(2)}) copy-start(bf16[16]{0:T(256)(128)(2,1)} %param.38) | copy-start | bytes 100
  9.5 132.8 %copy-start.31 = (bf16[16]{0:T(256)(128)(2,1)S(1)}, bf16[16]{0:T(256)(128)(2,1)}, u32[]{:S(2)}) copy-start(bf16[16]{0:T(256)(128)(2,1)} %param.37) | copy-start | bytes 100
  9.5 133.1 %copy-start.32 = (bf16[96]{0:T(256)(128)(2,1)S(1)}, bf16[96]{0:T(256)(128)(2,1)}, u32[]{:S(2)}) copy-start(bf16[96]{0:T(256)(128)(2,1)} %param.33) | copy-start | bytes 580
  9.5 256.9 %all-to-all-start.1 = ((bf16[64,32,512]{2,1,0:T(8,128)(2,1)}), bf16[64,32,512]{2,1,0:T(8,128)(2,1)}, u32[]{:S(2)}, u32[]{:S(2)}) async-start(bf16[64,32,512]{2,1,0:T(8,128)(2,1)} %param.39), calls=%async_computation.1 | async-start | bytes 4194304 | tf_op jit(solution)/shard_map/all_to_all | solution.py:249
  17.0 163.8 %copy-start.12 = (bf16[2,256,768]{2,1,0:T(8,128)(2,1)S(1)}, bf16[2,256,768]{2,1,0:T(8,128)(2,1)}, u32[]{:S(2)}) copy-start(bf16[2,256,768]{2,1,0:T(8,128)(2,1)} %param.22) | copy-start | bytes 2359300
  17.0 321.2 %all-gather.12.cloned.1.call-start = ((), (), s32[]{:S(2)}) async-start(), calls=%async_computation.10 | async-start | bytes 4866048 | tf_op jit(solution)/shard_map/all_gather | solution.py:194
  17.6 543.3 %all-reduce.21.cloned.1.call-start = ((), (), s32[]{:S(2)}) async-start(), calls=%async_computation.16 | async-start | bytes 786432
  281.4 67.3 %copy-start = (f32[512,768]{1,0:T(8,128)}, f32[512,768]{1,0:T(8,128)S(1)}, u32[]{:S(2)}) copy-start(f32[512,768]{1,0:T(8,128)S(1)} %fusion.18) | copy-start | bytes 4718596
  338.1 7.5 copy-start.3
  338.1 7.5 copy-start.23
  345.6 3.1 copy-start.33
  349.4 2.4 copy-start.5
  407.7 2.5 copy-start.10
  407.7 2.6 copy-start.6
  413.4 234.7 %reduce-scatter.14.cloned.1.call-start = ((), (), s32[]{:S(2)}) async-start(), calls=%async_computation.15 | async-start | bytes 1622016 | tf_op jit(solution)/shard_map/reduce_scatter | solution.py:348
  413.6 6.9 copy-start.7
  422.3 330.3 %reduce-scatter.8.cloned.1.call-start = ((), (), s32[]{:S(2)}) async-start(), calls=%async_computation.12 | async-start | bytes 2433024 | tf_op jit(solution)/shard_map/reduce_scatter | solution.py:341
  425.7 451.8 %reduce-scatter.6.cloned.1.call-start = ((), (), s32[]{:S(2)}) async-start(), calls=%async_computation.11 | async-start | bytes 7299072 | tf_op jit(solution)/shard_map/reduce_scatter | solution.py:340
  433.4 585.7 %reduce-scatter.10.cloned.1.call-start = ((), (), s32[]{:S(2)}) async-start(), calls=%async_computation.13 | async-start | bytes 9732096 | tf_op jit(solution)/shard_map/reduce_scatter | solution.py:344
  440.7 719.9 %reduce-scatter.12.cloned.1.call-start = ((), (), s32[]{:S(2)}) async-start(), calls=%async_computation.14 | async-start | bytes 9732096 | tf_op jit(solution)/shard_map/reduce_scatter | solution.py:346
  482.6 2.9 copy-start.8
  482.6 79.6 %all-to-all-start = ((bf16[2,1024,512]{2,0,1:T(2,128)(2,1)}), bf16[2,1024,512]{2,0,1:T(2,128)(2,1)S(1)}, u32[]{:S(2)}, u32[]{:S(2)}) async-start(bf16[2,1024,512]{2,0,1:T(2,128)(2,1)} %copy.125), calls=%async_computation | async-start | bytes 4194304 | tf_op jit(solution)/shard_map/all_to_all | solution.py:248
  (14 other events, 17.5 us)
Sparse Core Ops, SparseCore 0:
  10.8 73.5 all-gather.5
  87.2 52.7 all-gather.7
  142.8 64.1 all-gather.9
  209.7 63.5 all-gather.11
  413.5 131.6 all-reduce.20
  550.8 97.1 reduce-scatter.13
  653.9 98.6 reduce-scatter.7
  758.9 118.5 reduce-scatter.5
  883.9 135.0 reduce-scatter.9
  1025.4 135.1 reduce-scatter.11
where the time goes:
time: 1170 us
  waiting for transfers between devices  599 us (51%)
  blocking collectives  313 us (27%)
  local copies, waits for them, and re-layouts  133 us (11%)
  matrix products  80.3 us (7%)
  between operations  15.1 us (1%)
    reduce_scatter x1, waiting for transfers between devices, local(): lax.psum_scatter(local_grads[7], ('dp', 'fsdp'), scatter_dimension=0, til...  142 us
    reduce_scatter x1, waiting for transfers between devices, local(): lax.psum_scatter(local_grads[9], ('dp', 'fsdp'), scatter_dimension=0, til...  142 us
    reduce_scatter x1, waiting for transfers between devices, local(): lax.psum_scatter(local_grads[3], ('dp', 'fsdp'), scatter_dimension=0, til...  125 us
    all_gather x1, blocking collectives, local(): lax.all_gather(shards[0], ('dp', 'fsdp'), axis=0, tiled=True)  123 us
    unnamed x2, blocking collectives  106 us
    reduce_scatter x1, waiting for transfers between devices, local(): lax.psum_scatter(local_grads[4], ('dp', 'fsdp'), scatter_dimension=0, til...  105 us
    reduce_scatter x1, waiting for transfers between devices, local(): lax.psum_scatter(local_grads[11], ('dp', 'fsdp'), scatter_dimension=0, ti...  84 us
    all_gather x1, blocking collectives, local(): lax.all_gather(shards[11], ('dp', 'fsdp'), axis=0, tiled=True)  83.6 us
  transfers between devices with their start and end apart: 12, of which 5 were waited for; matrix products, arithmetic and copies ran while one was open for 12% of the time, Pallas kernels for 0%

commit v1 on v0

--- a/solution.py
+++ b/solution.py
@@ -12,6 +12,18 @@
 ROOT_HALF = 0.7071067811865476
 INVERSE_ROOT_TAU = 0.3989422804014327
 HIGH_PRECISION = lax.Precision.HIGHEST
+
+
+def gather_by_bits(x, axis, dim):
+    ways, here = (lax.axis_size(axis), lax.axis_index(axis))
+    grown, reach = (x, 1)
+    while reach < ways:
+        theirs = lax.ppermute(grown, axis, [(d, d ^ reach) for d in range(ways)])
+        mine_first = jnp.concatenate([grown, theirs], axis=dim)
+        theirs_first = jnp.concatenate([theirs, grown], axis=dim)
+        grown = jnp.where(here & reach == 0, mine_first, theirs_first)
+        reach = 2 * reach
+    return grown
 
 
 def product(left_op, right_op):
@@ -193,7 +205,7 @@
         lax.all_gather(shards[8], ("dp", "fsdp"), axis=0, tiled=True),
         lax.all_gather(shards[9], ("dp", "fsdp"), axis=0, tiled=True),
         lax.all_gather(shards[10], ("dp", "fsdp"), axis=0, tiled=True),
-        lax.all_gather(shards[11], ("dp", "fsdp"), axis=0, tiled=True),
+        gather_by_bits(shards[11], ("dp", "fsdp"), 0),
         lax.all_gather(shards[12], ("dp", "fsdp"), axis=0, tiled=True),
         lax.all_gather(shards[13], ("dp", "fsdp"), axis=0, tiled=True),
     )

time: 1170 us -> 1180 us (level)
    ppermute x0 -> x5, waiting for transfers between devices: none -> 25.8 us  [gather_by_bits(): theirs = lax.ppermute(grown, axis, [(d, d ^ reach) for d in range(ways)])]
    reduce_scatter x1, waiting for transfers between devices: 84 us -> 61.9 us  [local(): lax.psum_scatter(local_grads[11], ('dp', 'fsdp'), scatter_dimension=0, ti...]
  transfers between devices with their start and end apart: 12 -> 17, of which waited for: 5 -> 10; matrix products, arithmetic and copies ran while one was open for 12% -> 12% of each run, Pallas kernels for 0% -> 0%
where the time goes in v1:
time: 1180 us; the launch traced here: 1170 us
  waiting for transfers between devices  603 us (51%)
  blocking collectives  313 us (27%)
  local copies, waits for them, and re-layouts  132 us (11%)
  matrix products  80.5 us (7%)
  between operations  15.2 us (1%)
  starting transfers between devices  13.3 us (1%)
    reduce_scatter x1, waiting for transfers between devices, local(): lax.psum_scatter(local_grads[7], ('dp', 'fsdp'), scatter_dimension=0, til...  142 us
    reduce_scatter x1, waiting for transfers between devices, local(): lax.psum_scatter(local_grads[9], ('dp', 'fsdp'), scatter_dimension=0, til...  141 us
    reduce_scatter x1, waiting for transfers between devices, local(): lax.psum_scatter(local_grads[3], ('dp', 'fsdp'), scatter_dimension=0, til...  125 us
    all_gather x1, blocking collectives, local(): lax.all_gather(shards[0], ('dp', 'fsdp'), axis=0, tiled=True)  123 us
    unnamed x2, blocking collectives  106 us
    reduce_scatter x1, waiting for transfers between devices, local(): lax.psum_scatter(local_grads[4], ('dp', 'fsdp'), scatter_dimension=0, til...  105 us
    all_gather x1, blocking collectives, local(): lax.all_gather(shards[11], ('dp', 'fsdp'), axis=0, tiled=True)  83.8 us
    reduce_scatter x1, waiting for transfers between devices, local(): lax.psum_scatter(local_grads[11], ('dp', 'fsdp'), scatter_dimension=0, ti...  61.9 us
  transfers between devices with their start and end apart: 17, of which 10 were waited for; matrix products, arithmetic and copies ran while one was open for 12% of the time, Pallas kernels for 0%

profile of v1, /device:TPU:0, one launch (start us, length us, event | category | flops | bytes accessed | tf_op | source)
XLA Modules:
  0.0 1173.1 jit_solution(10549479731364341745)
XLA Ops:
  9.5 7.5 all-to-all-start.1
  17.7 123.0 %all-gather = bf16[32,4,768]{2,1,0:T(4,128)(2,1)S(1)} all-gather(bf16[1,4,768]{2,1,0:T(4,128)(2,1)S(1)} %bitcast.242), channel_id=1, replica_groups=mesh['dp'=8,'fsdp'=4] {'dp','fsdp'}, dimensions={0}, use_global_device_ids=true | all-gather | bytes 202752 | tf_op jit(solution)/shard_map/all_gather | solution.py:197
  142.8 37.7 %all-reduce.18 = (bf16[512]{0:T(512)(128)(2,1)S(1)}, bf16[768]{0:T(1024)(128)(2,1)S(1)}, bf16[768]{0:T(1024)(128)(2,1)S(1)}, bf16[768]{0:T(1024)(128)(2,1)S(1)},...) all-reduce(bf16[512]{0:T(512)(128)(2,1)S(1)} %dynamic-update-slice,, ...), channel_id=1, replica_groups=mesh['dp'=8,'fsdp'=4] {'dp','fsdp'}, use_global_device_ids=true, to_apply=%add | all-reduce | flops 7936 | bytes 31744
  182.8 83.8 %all_gather.61 = bf16[768,512]{1,0:T(8,128)(2,1)} all-gather(bf16[24,512]{1,0:T(8,128)(2,1)S(1)} %copy-done.18), channel_id=1, replica_groups=mesh['dp'=8,'fsdp'=4] {'dp','fsdp'}, dimensions={0}, use_global_device_ids=true | all-gather | bytes 811008 | tf_op jit(solution)/shard_map/all_gather | solution.py:274
  266.6 3.2 copy.128
  269.7 9.9 gather_fusion
  281.6 4.8 convolution_convert_fusion.1
  294.8 28.2 %while.30 = (s32[]{:T(128)}, bf16[6,2,256,128]{2,3,1,0:T(8,128)(2,1)}, f32[6,2,2,256,1]{3,2,1,4,0:T(2,128)S(1)}, s32[6]{0:T(128)S(1)}, bf16[2,256,768]{1,2,0:T(8...) while((s32[]{:T(128)}, ...), condition=%wide.region_6.7_spmd, body=%wide.region_3.6_spmd.sunk | while | flops 69008384 | bytes 4751551 | solution.py:103
  326.1 2.4 fusion.43
  330.0 8.4 multiply_convert_fusion.1
  338.4 7.5 convert_reduce_fusion
  345.9 3.1 multiply_reduce_fusion.1
  352.1 49.0 %while.31 = (s32[]{:T(128)}, bf16[6,2,256,128]{2,3,1,0:T(8,128)(2,1)}, bf16[6,2,256,128]{2,3,1,0:T(8,128)(2,1)}, bf16[6,2,256,128]{2,3,1,0:T(8,128)(2,1)}, s32[6...) while((s32[]{:T(128)}, ...), condition=%wide.region_14.15_spmd, body=%wide.region_12.14_spmd.sunk | while | flops 170130432 | bytes 11292899 | solution.py:149
  408.1 2.5 multiply_reduce_fusion.2
  414.0 6.0 add_convert_fusion
  422.8 3.3 fusion.20
  427.2 6.6 fusion.45
  433.9 7.2 fusion.39
  442.6 8.2 fusion.33
  450.9 3.8 collective-permute-done
  454.8 5.0 collective-permute-done.1
  461.3 7.0 collective-permute-done.3
  470.3 8.6 collective-permute-done.4
  479.7 26.7 %scatter_fusion = bf16[2,1024,512]{2,1,0:T(8,128)(2,1)S(1)} fusion(bf16[2,1024,512]{2,1,0:T(8,128)(2,1)S(1)} %broadcast_in_dim.84, s32[512]{0:T(512)S(1)} %bitcast.199, bf16[512,512]{1,0:T(8,128)(2,1)S(1)} %fusion.12), kind=kCustom, calls=%fused_computation.1 | custom fusion | bytes 1576960 | tf_op jit(solution)/shard_map/scatter | solution.py:259
  506.5 3.5 copy.125
  509.9 2.9 all-to-all-start
  515.0 68.7 %all-reduce.17 = (f32[768]{0:T(1024)S(1)}, f32[768]{0:T(1024)S(1)}, f32[768]{0:T(1024)S(1)}, f32[768]{0:T(1024)S(1)}, f32[3072]{0:T(1024)S(1)}, /*index=5*/f32[768]{0:T(1024)S(1)}, f32[512]{0:T(512)S(1)}, f32[512]{0:T(512)S(1)}) all-reduce(f32[768]{0:T(1024)S(1)} %get-tuple-element.342, ...), channel_id=3, replica_groups=mesh['dp'=8,'fsdp'=4] {'dp','fsdp'}, use_global_device_ids=true, to_apply=%region_20.21.clone | all-reduce | flops 7936 | bytes 63488
  591.6 61.9 %reduce-scatter.14.cloned.1.call-done = f32[24,512]{1,0:T(8,128)} async-done(((f32[768,512]{1,0:T(8,128)}), f32[24,512]{1,0:T(8,128)}) %reduce-scatter.14.cloned.1.call-update) | async-done | bytes 49168 | tf_op jit(solution)/shard_map/reduce_scatter | solution.py:360
  653.5 104.5 %reduce-scatter.8.cloned.1.call-done = f32[24,768]{1,0:T(8,128)} async-done(((f32[768,768]{1,0:T(8,128)}), f32[24,768]{1,0:T(8,128)}) %reduce-scatter.8.cloned.1.call-update) | async-done | bytes 73744 | tf_op jit(solution)/shard_map/reduce_scatter | solution.py:353
  758.1 124.8 %reduce-scatter.6.cloned.1.call-done = f32[24,2304]{1,0:T(8,128)} async-done(((f32[768,2304]{1,0:T(8,128)}), f32[24,2304]{1,0:T(8,128)}) %reduce-scatter.6.cloned.1.call-update) | async-done | bytes 221200 | tf_op jit(solution)/shard_map/reduce_scatter | solution.py:352
  882.9 141.6 %reduce-scatter.10.cloned.1.call-done = f32[24,3072]{1,0:T(8,128)} async-done(((f32[768,3072]{1,0:T(8,128)}), f32[24,3072]{1,0:T(8,128)}) %reduce-scatter.10.cloned.1.call-update) | async-done | bytes 294928 | tf_op jit(solution)/shard_map/reduce_scatter | solution.py:356
  1024.5 141.4 %reduce-scatter.12.cloned.1.call-done = f32[96,768]{1,0:T(8,128)} async-done(((f32[3072,768]{1,0:T(8,128)}), f32[96,768]{1,0:T(8,128)}) %reduce-scatter.12.cloned.1.call-update) | async-done | bytes 294928 | tf_op jit(solution)/shard_map/reduce_scatter | solution.py:358
  (331 shorter events, 123.8 us)
Async XLA Ops:
  7.2 274.4 %all-gather.6.cloned.1.call-start = ((), (), s32[]{:S(2)}) async-start(), calls=%async_computation.7 | async-start | bytes 3649536 | tf_op jit(solution)/shard_map/all_gather | solution.py:200
  7.9 318.2 %all-gather.8.cloned.1.call-start = ((), (), s32[]{:S(2)}) async-start(), calls=%async_computation.8 | async-start | bytes 1216512 | tf_op jit(solution)/shard_map/all_gather | solution.py:201
  8.7 321.3 %all-gather.10.cloned.1.call-start = ((), (), s32[]{:S(2)}) async-start(), calls=%async_computation.9 | async-start | bytes 4866048 | tf_op jit(solution)/shard_map/all_gather | solution.py:204
  9.4 8.3 copy-start.20
  9.4 131.4 %copy-start.21 = (s32[2,13]{1,0:T(2,128)S(1)}, s32[2,13]{1,0:T(2,128)}, u32[]{:S(2)}) copy-start(s32[2,13]{1,0:T(2,128)} %param.23) | copy-start | bytes 316
  9.4 131.5 %copy-start.24 = (bf16[24]{0:T(256)(128)(2,1)S(1)}, bf16[24]{0:T(256)(128)(2,1)}, u32[]{:S(2)}) copy-start(bf16[24]{0:T(256)(128)(2,1)} %param.27) | copy-start | bytes 148
  9.4 131.7 %copy-start.25 = (bf16[24]{0:T(256)(128)(2,1)S(1)}, bf16[24]{0:T(256)(128)(2,1)}, u32[]{:S(2)}) copy-start(bf16[24]{0:T(256)(128)(2,1)} %param.26) | copy-start | bytes 148
  9.4 131.9 %copy-start.26 = (bf16[24]{0:T(256)(128)(2,1)S(1)}, bf16[24]{0:T(256)(128)(2,1)}, u32[]{:S(2)}) copy-start(bf16[24]{0:T(256)(128)(2,1)} %param.31) | copy-start | bytes 148
  9.4 132.1 %copy-start.27 = (bf16[24]{0:T(256)(128)(2,1)S(1)}, bf16[24]{0:T(256)(128)(2,1)}, u32[]{:S(2)}) copy-start(bf16[24]{0:T(256)(128)(2,1)} %param.30) | copy-start | bytes 148
  9.5 132.4 %copy-start.28 = (bf16[24]{0:T(256)(128)(2,1)S(1)}, bf16[24]{0:T(256)(128)(2,1)}, u32[]{:S(2)}) copy-start(bf16[24]{0:T(256)(128)(2,1)} %param.35) | copy-start | bytes 148
  9.5 132.6 %copy-start.29 = (bf16[16]{0:T(256)(128)(2,1)S(1)}, bf16[16]{0:T(256)(128)(2,1)}, u32[]{:S(2)}) copy-start(bf16[16]{0:T(256)(128)(2,1)} %param.38) | copy-start | bytes 100
  9.5 132.8 %copy-start.30 = (bf16[16]{0:T(256)(128)(2,1)S(1)}, bf16[16]{0:T(256)(128)(2,1)}, u32[]{:S(2)}) copy-start(bf16[16]{0:T(256)(128)(2,1)} %param.37) | copy-start | bytes 100
  9.5 133.1 %copy-start.31 = (bf16[96]{0:T(256)(128)(2,1)S(1)}, bf16[96]{0:T(256)(128)(2,1)}, u32[]{:S(2)}) copy-start(bf16[96]{0:T(256)(128)(2,1)} %param.33) | copy-start | bytes 580
  9.5 257.1 %all-to-all-start.1 = ((bf16[64,32,512]{2,1,0:T(8,128)(2,1)}), bf16[64,32,512]{2,1,0:T(8,128)(2,1)}, u32[]{:S(2)}, u32[]{:S(2)}) async-start(bf16[64,32,512]{2,1,0:T(8,128)(2,1)} %param.39), calls=%async_computation.1 | async-start | bytes 4194304 | tf_op jit(solution)/shard_map/all_to_all | solution.py:261
  17.0 163.8 %copy-start.12 = (bf16[2,256,768]{2,1,0:T(8,128)(2,1)S(1)}, bf16[2,256,768]{2,1,0:T(8,128)(2,1)}, u32[]{:S(2)}) copy-start(bf16[2,256,768]{2,1,0:T(8,128)(2,1)} %param.22) | copy-start | bytes 2359300
  17.0 321.4 %all-gather.12.cloned.1.call-start = ((), (), s32[]{:S(2)}) async-start(), calls=%async_computation.10 | async-start | bytes 4866048 | tf_op jit(solution)/shard_map/all_gather | solution.py:206
  17.6 570.8 %all-reduce.21.cloned.1.call-start = ((), (), s32[]{:S(2)}) async-start(), calls=%async_computation.16 | async-start | bytes 786432
  281.6 67.4 %copy-start = (f32[512,768]{1,0:T(8,128)}, f32[512,768]{1,0:T(8,128)S(1)}, u32[]{:S(2)}) copy-start(f32[512,768]{1,0:T(8,128)S(1)} %fusion.24) | copy-start | bytes 4718596
  338.4 7.5 copy-start.3
  338.4 7.5 copy-start.22
  413.8 239.8 %reduce-scatter.14.cloned.1.call-start = ((), (), s32[]{:S(2)}) async-start(), calls=%async_computation.15 | async-start | bytes 1622016 | tf_op jit(solution)/shard_map/reduce_scatter | solution.py:360
  422.7 335.3 %reduce-scatter.8.cloned.1.call-start = ((), (), s32[]{:S(2)}) async-start(), calls=%async_computation.12 | async-start | bytes 2433024 | tf_op jit(solution)/shard_map/reduce_scatter | solution.py:353
  426.1 456.8 %reduce-scatter.6.cloned.1.call-start = ((), (), s32[]{:S(2)}) async-start(), calls=%async_computation.11 | async-start | bytes 7299072 | tf_op jit(solution)/shard_map/reduce_scatter | solution.py:352
  433.9 590.6 %reduce-scatter.10.cloned.1.call-start = ((), (), s32[]{:S(2)}) async-start(), calls=%async_computation.13 | async-start | bytes 9732096 | tf_op jit(solution)/shard_map/reduce_scatter | solution.py:356
  441.2 724.8 %reduce-scatter.12.cloned.1.call-start = ((), (), s32[]{:S(2)}) async-start(), calls=%async_computation.14 | async-start | bytes 9732096 | tf_op jit(solution)/shard_map/reduce_scatter | solution.py:358
  450.8 28.2 %copy-start.17 = (bf16[512,768]{1,0:T(8,128)(2,1)S(1)}, bf16[512,768]{1,0:T(8,128)(2,1)}, u32[]{:S(2)}) copy-start(bf16[512,768]{1,0:T(8,128)(2,1)} %copy-done.16) | copy-start | bytes 2359300
  450.8 3.9 collective-permute-start
  454.7 5.1 collective-permute-start.1
  459.8 1.4 collective-permute-start.2
  461.2 7.1 collective-permute-start.3
  468.5 10.5 collective-permute-start.4
  509.9 79.8 %all-to-all-start = ((bf16[2,1024,512]{2,0,1:T(2,128)(2,1)}), bf16[2,1024,512]{2,0,1:T(2,128)(2,1)S(1)}, u32[]{:S(2)}, u32[]{:S(2)}) async-start(bf16[2,1024,512]{2,0,1:T(2,128)(2,1)} %copy.125), calls=%async_computation | async-start | bytes 4194304 | tf_op jit(solution)/shard_map/all_to_all | solution.py:260
  (18 other events, 35.4 us)
Sparse Core Ops, SparseCore 0:
  10.8 73.5 all-gather.5
  87.2 52.7 all-gather.7
  142.8 64.1 all-gather.9
  209.7 63.4 all-gather.11
  413.9 136.1 all-reduce.20
  555.8 97.7 reduce-scatter.13
  659.4 98.6 reduce-scatter.7
  764.3 118.5 reduce-scatter.5
  889.4 135.0 reduce-scatter.9
  1030.8 135.0 reduce-scatter.11
